TPU v7x, 32 devices: a whole 2x2x4 slice. The times are simulated.
32 devices in a mesh: section: 2 (over x), mp: 4 (over z), dp: 4 (over y, core).
Axes of the slice: x: 2, y: 2, z: 4, core: 2. Of those that a mesh axis runs over, the one named last changes fastest.
Arguments:
- text_in: bfloat16 [4, 2, 512, 8192], P('dp', 'section', None, 'mp'), may hold values from -6 to 6
- vision: bfloat16 [4, 2, 256, 8192], P('dp', 'section', None, 'mp'), may hold values from -6 to 6
- tile_counts: int32 [4, 2], P('dp'), may hold values from 1 to 4, as said below
- lengths: int32 [4, 2], P('dp', 'section'), may hold values from 128 to 512, as said below
- image_of: int32 [4, 2], P('dp'), may hold values from 0 to 1, each once within a row
- norm_gain: float32 [2, 8192], P('section'), may hold values from 0.5 to 1.5
- query_weight: bfloat16 [2, 8192, 4096], P('section', 'dp', 'mp'), may hold values from -0.0625 to 0.0625
- key_weight: bfloat16 [2, 8192, 1024], P('section', 'dp', 'mp'), may hold values from -0.0625 to 0.0625
- value_weight: bfloat16 [2, 8192, 1024], P('section', 'dp', 'mp'), may hold values from -0.0625 to 0.0625
- query_gain: float32 [2, 128], P('section')
- key_gain: float32 [2, 128], P('section')
- cross_gate: float32 [2], P('section'), may hold values from 0.4 to 1.5
- context_grad: bfloat16 [4, 2, 512, 4096], P('dp', 'section', None, 'mp'), may hold values from -6 to 6
Outputs:
- gated_context: bfloat16 [4, 2, 512, 4096], P('dp', 'section', None, 'mp')
- vision_grad: bfloat16 [4, 2, 256, 8192], P('dp', 'section', None, 'mp')
- key_weight_grad: bfloat16 [2, 8192, 1024], P('section', 'dp', 'mp')
- value_weight_grad: bfloat16 [2, 8192, 1024], P('section', 'dp', 'mp')
Inputs may be any that keep to these rules, and one draw needn't show every extreme that they name: `tile_counts`: some image has 4 tiles and some has one. `lengths`: some sample has the full 512 tokens. `image_of`: each row is a permutation of the sections.
All inputs are finite; a program needn't handle non-finite values.
Results may differ from a plain program's by a relative error of at most 0.018.
Values may be sent and summed in bfloat16 or wider, within the bound.
No kernel may reach another device: no remote copies, remote signals or barrier semaphores. Data moves between devices by JAX's collectives and lax.ppermute only.
A program may use at most 192 MiB of HBM per device.

v0:
```python
import jax
import jax.numpy as jnp
from jax import lax
from jax.sharding import PartitionSpec as P

HD = 128
TILE_ROWS = 64


def shifted(value, axis, steps):
    count = lax.axis_size(axis)
    pairs = [(source, (source + steps) % count) for source in range(count)]
    return lax.ppermute(value, axis, pairs)


def norm_rows(values, gain):
    values = values.astype(jnp.float32)
    scaled = values * lax.rsqrt(jnp.mean(values * values, axis=-1, keepdims=True) + 1e-05)
    return scaled * gain


def rounded(values):
    return lax.optimization_barrier(values.astype(jnp.bfloat16)).astype(jnp.float32)


def attend(queries, keys_raw, values_raw, key_norm, usable, present, gate_value):
    keys = rounded(norm_rows(keys_raw, key_norm))
    values = rounded(values_raw)
    text_rows, heads, depth = queries.shape
    groups = keys.shape[1]
    grouped = queries.astype(jnp.float32).reshape(text_rows, groups, heads // groups, depth)
    scores = jnp.einsum("tgjd,vgd->gjtv", grouped, keys) * depth ** (-0.5)
    scores = jnp.where(usable[None, None, None, :], scores, -1e30)
    highest = lax.stop_gradient(jnp.max(scores, axis=-1, keepdims=True))
    weights = jnp.exp(scores - highest)
    probs = rounded(weights / jnp.sum(weights, axis=-1, keepdims=True))
    context = jnp.einsum("gjtv,vgd->tgjd", probs, values).reshape(text_rows, heads * depth)
    return jnp.where(present[:, None], jnp.tanh(gate_value) * context, 0.0)


def per_device(
    text_in,
    vision,
    tile_counts,
    lengths,
    image_of,
    norm_gain,
    query_weight,
    key_weight,
    value_weight,
    query_gain,
    key_gain,
    cross_gate,
    context_grad,
):
    arrived = shifted(text_in, "section", 1)
    full_text = lax.all_gather(arrived, "mp", axis=3, tiled=True)[0, 0]
    text_rows = full_text.shape[0]
    normed = norm_rows(full_text, norm_gain[0]).astype(jnp.bfloat16)
    width_q = query_weight.shape[2]
    columns = normed
    query_raw = jnp.dot(
        columns,
        lax.all_gather(query_weight, "dp", axis=1, tiled=True)[0],
        preferred_element_type=jnp.float32,
    )
    queries = norm_rows(query_raw.reshape(text_rows, width_q // HD, HD), query_gain[0]).astype(
        jnp.bfloat16
    )
    key_full, value_full = (
        lax.all_gather(key_weight, "dp", axis=1, tiled=True),
        lax.all_gather(value_weight, "dp", axis=1, tiled=True),
    )
    key_full = key_full[0]
    value_full = value_full[0]
    slot_rows = vision.shape[2]
    part_width = vision.shape[3]
    wanted = image_of[0, lax.axis_index("section")]
    shard_piece = lax.all_gather(vision, "section", axis=1, tiled=True)
    owners = jnp.arange(shard_piece.shape[1])
    chosen = (owners == wanted)[:, None, None]
    taken = jnp.where(chosen, shard_piece[0], jnp.zeros_like(shard_piece[0]))
    image_part = jnp.sum(taken.astype(jnp.float32), axis=0).astype(jnp.bfloat16)
    image = lax.all_gather(image_part, "mp", axis=1, tiled=True)
    width_k = key_full.shape[1]
    keys_raw = jnp.dot(image, key_full, preferred_element_type=jnp.float32).reshape(
        slot_rows, width_k // HD, HD
    )
    values_raw = jnp.dot(image, value_full, preferred_element_type=jnp.float32).reshape(
        slot_rows, width_k // HD, HD
    )
    usable = jnp.arange(slot_rows) < tile_counts[0, wanted] * TILE_ROWS
    present = jnp.arange(text_rows) < lengths[0, 0]

    def forward(keys_in, values_in):
        return attend(queries, keys_in, values_in, key_gain[0], usable, present, cross_gate[0])

    context, pullback = jax.vjp(forward, keys_raw, values_raw)
    gated_context = context.astype(jnp.bfloat16).reshape(1, 1, text_rows, width_q)
    key_back, value_back = pullback(context_grad[0, 0].astype(jnp.float32))
    key_flat = key_back.reshape(slot_rows, width_k).astype(jnp.bfloat16)
    value_flat = value_back.reshape(slot_rows, width_k).astype(jnp.bfloat16)
    contract = (((1,), (1,)), ((), ()))
    partial_sum = lax.dot_general(key_flat, key_full, contract, preferred_element_type=jnp.float32)
    partial_sum = partial_sum + lax.dot_general(
        value_flat, value_full, contract, preferred_element_type=jnp.float32
    )
    partial_bf = partial_sum.astype(jnp.bfloat16)
    summed = lax.psum_scatter(
        partial_bf.astype(jnp.float32).astype(jnp.bfloat16), "mp", scatter_dimension=1, tiled=True
    )
    row_ids = jnp.arange(slot_rows * lax.axis_size("section"))
    taken = jnp.take(summed, row_ids % slot_rows, axis=0).astype(jnp.float32)
    routed = lax.psum_scatter(
        jnp.where((row_ids // slot_rows == wanted)[:, None], taken, 0.0).astype(jnp.bfloat16),
        "section",
        scatter_dimension=0,
        tiled=True,
    )
    vision_grad = routed.reshape(1, 1, slot_rows, part_width)
    columns = image
    inner = (((0,), (0,)), ((), ()))
    key_part = lax.dot_general(columns, key_flat, inner, preferred_element_type=jnp.float32).astype(
        jnp.bfloat16
    )
    value_part = lax.dot_general(
        columns, value_flat, inner, preferred_element_type=jnp.float32
    ).astype(jnp.bfloat16)
    both_grads = lax.psum_scatter(
        jnp.concatenate([key_part, value_part], axis=1).astype(jnp.float32).astype(jnp.bfloat16),
        "dp",
        scatter_dimension=0,
        tiled=True,
    )
    key_weight_grad = both_grads[:, :width_k][None]
    value_weight_grad = both_grads[:, width_k:][None]
    return (gated_context, vision_grad, key_weight_grad, value_weight_grad)


def solution(mesh):
    return jax.shard_map(
        per_device,
        mesh=mesh,
        in_specs=(
            P("dp", "section", None, "mp"),
            P("dp", "section", None, "mp"),
            P("dp", None),
            P("dp", "section"),
            P("dp", None),
            P("section", None),
            P("section", "dp", "mp"),
            P("section", "dp", "mp"),
            P("section", "dp", "mp"),
            P("section", None),
            P("section", None),
            P("section"),
            P("dp", "section", None, "mp"),
        ),
        out_specs=(
            P("dp", "section", None, "mp"),
            P("dp", "section", None, "mp"),
            P("section", "dp", "mp"),
            P("section", "dp", "mp"),
        ),
        check_vma=False,
    )
```

profile of v0, /device:TPU:0, one launch (start us, length us, event | category | flops | bytes accessed | tf_op | source)
XLA Modules:
  0.0 705.0 jit_solution(10474390815657424555)
XLA Ops:
  10.7 34.7 %all-gather.7.cloned.1.call-done = bf16[1,2,256,2048]{3,2,0,1:T(8,128)(2,1)} async-done(((bf16[1,1,256,2048]{3,2,0,1:T(8,128)(2,1)}), bf16[1,2,256,2048]{3,2,0,1:T(8,128)(2,1)}) %all-gather.7.cloned.1.call-update) | async-done | bytes 2097168 | tf_op jit(solution)/shard_map/all_gather | solution.py:79
  45.4 3.4 fusion.34
  49.3 47.3 %collective-permute-done = bf16[1,1,512,2048]{3,2,1,0:T(8,128)(2,1)S(1)} collective-permute-done((bf16[1,1,512,2048]{3,2,1,0:T(8,128)(2,1)}, bf16[1,1,512,2048]{3,2,1,0:T(8,128)(2,1)S(1)}, u32[]{:S(2)}, u32[]{:S(2)}) %collective-permute-start) | collective-permute-done | bytes 2097184 | tf_op jit(solution)/shard_map/ppermute | solution.py:13
  96.5 1.4 copy-done.11
  104.2 6.4 copy.51
  110.6 7.0 all-gather.11.cloned.1.call-done
  117.6 6.4 copy.50
  123.9 76.4 %all-gather.9.cloned.1.call-done = bf16[256,8192]{1,0:T(8,128)(2,1)} async-done(((bf16[256,2048]{1,0:T(8,128)(2,1)}), bf16[256,8192]{1,0:T(8,128)(2,1)}) %all-gather.9.cloned.1.call-update) | async-done | bytes 4194320 | tf_op jit(solution)/shard_map/all_gather | solution.py:84
  200.4 4.9 multiply_reduce_fusion.2
  206.3 1.3 fusion.60
  207.6 2.0 fusion.43
  209.6 140.3 %all-gather.15.cloned.1.call-done = bf16[1,1,512,8192]{3,2,1,0:T(8,128)(2,1)} async-done(((bf16[1,1,512,2048]{3,2,1,0:T(8,128)(2,1)}), bf16[1,1,512,8192]{3,2,1,0:T(8,128)(2,1)}) %all-gather.15.cloned.1.call-update) | async-done | bytes 8388624 | tf_op jit(solution)/shard_map/all_gather | solution.py:57
  350.0 5.1 fusion.1
  355.1 100.4 %all-gather.17.cloned.1.call-done = bf16[1,8192,1024]{2,1,0:T(8,128)(2,1)} async-done(((bf16[1,2048,1024]{2,1,0:T(8,128)(2,1)}), bf16[1,8192,1024]{2,1,0:T(8,128)(2,1)}) %all-gather.17.cloned.1.call-update) | async-done | bytes 16777232 | tf_op jit(solution)/shard_map/all_gather | solution.py:64
  455.5 21.4 %copy.52 = bf16[1024,8192]{1,0:T(8,128)(2,1)} copy(bf16[1024,8192]{0,1:T(8,128)(2,1)} %bitcast.150) | data formatting | bytes 33554432 | tf_op jit(solution)/shard_map/dot_general | solution.py:62
  477.0 14.8 %multiply_reduce_fusion = (f32[512,8]{0,1:T(8,128)S(1)}, f32[512,8,128]{0,2,1:T(8,128)S(1)}) fusion(bf16[8,128,8192]{2,1,0:T(8,128)(2,1)} %bitcast.151, bf16[1,1,512,8192]{3,2,1,0:T(8,128)(2,1)} %all-gather.15.cloned.1.call-done, f32[8192]{0:T(1024)S(1)} %bitcast.169, f32[512]{0:T(512)S(1)} %add_rsqrt_fusion.1), kind=kOutput, calls=%fused_computation.55 | convolution fusion | flops 8607756288 | bytes 27314176 | tf_op jit(solution)/shard_map/dot_general | solution.py:62
  492.3 5.1 fusion.101
  498.1 3.9 fusion.16
  506.2 1.3 fusion.19
  508.4 3.4 fusion.4
  511.9 5.5 convolution_convert_fusion
  517.4 3.2 convolution_convert_fusion.1
  520.6 7.7 %pad_maximum_fusion = bf16[8192,512]{0,1:T(8,128)(2,1)} fusion(bf16[8192,256]{0,1:T(8,128)(2,1)} %convolution_convert_fusion, bf16[8192,256]{0,1:T(8,128)(2,1)} %convolution_convert_fusion.1), kind=kLoop, calls=%fused_computation.13 | loop fusion | flops 16777216 | bytes 16777216 | tf_op jit(solution)/shard_map/concatenate | solution.py:130
  529.1 59.6 %reduce-scatter.4.cloned.1.call-done = bf16[256,2048]{1,0:T(8,128)(2,1)} async-done(((bf16[256,8192]{1,0:T(8,128)(2,1)}), bf16[256,2048]{1,0:T(8,128)(2,1)}) %reduce-scatter.4.cloned.1.call-update) | async-done | bytes 1048592 | tf_op jit(solution)/shard_map/reduce_scatter | solution.py:109
  588.7 6.8 gather_fusion
  595.5 3.7 select_convert_fusion
  600.3 1.2 select_convert_fusion.1
  601.6 62.2 %reduce-scatter.8.cloned.1.call-done = bf16[2048,512]{0,1:T(8,128)(2,1)} async-done(((bf16[8192,512]{0,1:T(8,128)(2,1)}), bf16[2048,512]{0,1:T(8,128)(2,1)}) %reduce-scatter.8.cloned.1.call-update) | async-done | bytes 2097168 | tf_op jit(solution)/shard_map/reduce_scatter | solution.py:129
  663.8 1.7 slice_bitcast_fusion
  665.4 1.3 copy.64
  666.7 1.3 copy.65
  668.0 30.4 %reduce-scatter.6.cloned.1.call-done = bf16[256,2048]{1,0:T(8,128)(2,1)} async-done(((bf16[512,2048]{1,0:T(8,128)(2,1)}), bf16[256,2048]{1,0:T(8,128)(2,1)}) %reduce-scatter.6.cloned.1.call-update) | async-done | bytes 1048592 | tf_op jit(solution)/shard_map/reduce_scatter | solution.py:114
  (81 shorter events, 15.9 us)
Async XLA Ops:
  7.2 2.3 copy-start
  7.2 38.2 %all-gather.7.cloned.1.call-start = ((), (), s32[]{:S(2)}) async-start(), calls=%async_computation.3 | async-start | bytes 3145728 | tf_op jit(solution)/shard_map/all_gather | solution.py:79
  7.9 96.3 %all-gather.13.cloned.1.call-start = ((), (), s32[]{:S(2)}) async-start(), calls=%async_computation.6 | async-start | bytes 5242880 | tf_op jit(solution)/shard_map/all_gather | solution.py:71
  8.7 108.9 %all-gather.11.cloned.1.call-start = ((), (), s32[]{:S(2)}) async-start(), calls=%async_computation.5 | async-start | bytes 5242880 | tf_op jit(solution)/shard_map/all_gather | solution.py:72
  9.4 191.0 %all-gather.9.cloned.1.call-start = ((), (), s32[]{:S(2)}) async-start(), calls=%async_computation.4 | async-start | bytes 5242880 | tf_op jit(solution)/shard_map/all_gather | solution.py:84
  48.8 51.1 %copy-start.12 = (bf16[1,1,512,1024]{3,2,1,0:T(8,128)(2,1)S(1)}, bf16[1,1,512,1024]{3,2,1,0:T(8,128)(2,1)}, u32[]{:S(2)}) copy-start(bf16[1,1,512,1024]{3,2,1,0:T(8,128)(2,1)} %param.25) | copy-start | bytes 3145732
  48.8 301.2 %all-gather.15.cloned.1.call-start = ((), (), s32[]{:S(2)}) async-start(), calls=%async_computation.7 | async-start | bytes 10485760 | tf_op jit(solution)/shard_map/all_gather | solution.py:57
  48.9 47.6 %collective-permute-start = (bf16[1,1,512,2048]{3,2,1,0:T(8,128)(2,1)}, bf16[1,1,512,2048]{3,2,1,0:T(8,128)(2,1)S(1)}, u32[]{:S(2)}, u32[]{:S(2)}) collective-permute-start(bf16[1,1,512,2048]{3,2,1,0:T(8,128)(2,1)} %param.13), channel_id=1, source_target_pairs={{0,16},{16,0},{1,17},{17,1},{2,18},{18,2},{3,19},{19,3},{4,20},{20... | collective-permute-start | bytes 6291464 | tf_op jit(solution)/shard_map/ppermute | solution.py:13
  96.5 1.4 copy-start.11
  97.9 4.5 copy-start.17
  98.0 357.6 %all-gather.17.cloned.1.call-start = ((), (), s32[]{:S(2)}) async-start(), calls=%async_computation.8 | async-start | bytes 20971520 | tf_op jit(solution)/shard_map/all_gather | solution.py:64
  98.5 490.2 %reduce-scatter.4.cloned.1.call-start = ((), (), s32[]{:S(2)}) async-start(), calls=%async_computation.9 | async-start | bytes 5242880 | tf_op jit(solution)/shard_map/reduce_scatter | solution.py:109
  200.4 4.9 copy-start.14
  200.4 5.7 copy-start.5
  200.4 5.9 copy-start.10
  455.5 21.4 %copy-start.16 = (f32[1,8192]{1,0:T(1,128)S(1)}, f32[1,8192]{1,0:T(1,128)}, u32[]{:S(2)}) copy-start(f32[1,8192]{1,0:T(1,128)} %param.18) | copy-start | bytes 98308
  477.0 14.8 %copy-start.15 = (f32[1,128]{1,0:T(1,128)S(1)}, f32[1,128]{1,0:T(1,128)}, u32[]{:S(2)}) copy-start(f32[1,128]{1,0:T(1,128)} %param.22) | copy-start | bytes 1540
  498.1 3.9 copy-start.8
  498.1 4.7 copy-start.9
  498.1 4.7 copy-start.13
  498.1 4.7 copy-start.18
  502.0 2.3 copy-start.2
  504.0 2.2 copy-start.4
  506.2 2.2 copy-start.7
  511.8 151.9 %reduce-scatter.8.cloned.1.call-start = ((), (), s32[]{:S(2)}) async-start(), calls=%async_computation.11 | async-start | bytes 10485760 | tf_op jit(solution)/shard_map/reduce_scatter | solution.py:129
  511.9 5.5 copy-start.6
  528.3 170.1 %reduce-scatter.6.cloned.1.call-start = ((), (), s32[]{:S(2)}) async-start(), calls=%async_computation.10 | async-start | bytes 3145728 | tf_op jit(solution)/shard_map/reduce_scatter | solution.py:114
  595.5 3.7 copy-start.3
  600.3 98.1 %copy-start.1 = (s32[1,2]{1,0:T(1,128)S(1)}, s32[1,2]{1,0:T(1,128)}, u32[]{:S(2)}) copy-start(s32[1,2]{1,0:T(1,128)} %param.17) | copy-start | bytes 28
Sparse Core Ops, SparseCore 0:
  9.6 35.7 all-gather.6
  47.0 34.4 all-gather.12
  83.1 34.4 all-gather.10
  119.6 80.7 all-gather.8
  201.8 148.1 all-gather.14
  351.4 104.1 all-gather.16
  511.9 76.7 reduce-scatter.3
  591.5 72.2 reduce-scatter.7
  666.6 31.8 reduce-scatter.5
where the time goes:
time: 706 us; the launch traced here: 705 us
  waiting for transfers between devices  561 us (79%)
  local copies, waits for them, and re-layouts  51.3 us (7%)
  matrix products  44.1 us (6%)
  other arithmetic  30.3 us (4%)
  between operations  17.4 us (2%)
    all_gather x1, waiting for transfers between devices, per_device(): full_text = lax.all_gather(arrived, 'mp', axis=3, tiled=True)[0, 0]  140 us
    all_gather x1, waiting for transfers between devices, per_device(): lax.all_gather(query_weight, 'dp', axis=1, tiled=True)[0]  100 us
    all_gather x1, waiting for transfers between devices, per_device(): image = lax.all_gather(image_part, 'mp', axis=1, tiled=True)  76.4 us
    reduce_scatter x1, waiting for transfers between devices, per_device(): lax.psum_scatter(jnp.concatenate([key_part, value_part], axis=1).astype(j...  62.2 us
    reduce_scatter x1, waiting for transfers between devices, per_device(): lax.psum_scatter(partial_bf.astype(jnp.float32).astype(jnp.bfloat16), 'mp...  59.6 us
    ppermute x1, waiting for transfers between devices, shifted(): return lax.ppermute(value, axis, pairs)  47.3 us
    all_gather x1, waiting for transfers between devices, per_device(): shard_piece = lax.all_gather(vision, 'section', axis=1, tiled=True)  34.7 us
    reduce_scatter x1, waiting for transfers between devices, per_device(): lax.psum_scatter(jnp.where((row_ids // slot_rows == wanted)[:, None], tak...  30.4 us
  transfers between devices with their start and end apart: 10, of which 9 were waited for; matrix products, arithmetic and copies ran while one was open for 10% of the time, Pallas kernels for 0%

commit v1 on v0

--- a/solution.py
+++ b/solution.py
@@ -1,10 +1,28 @@
+import functools
 import jax
 import jax.numpy as jnp
 from jax import lax
 from jax.sharding import PartitionSpec as P
+from jax.lax import axis_index, axis_size, ppermute
 
 HD = 128
 TILE_ROWS = 64
+
+
+def tiles_bind(shard_in, mesh_dim):
+    slots = axis_size(mesh_dim)
+    left_arr = [(t - 1, t) for t in range(1, slots)] + [(slots - 1, 0)]
+    z = shard_in
+    fields = [z]
+    for _ in tuple(range(slots - 1)):
+        z = ppermute(z, mesh_dim, perm=left_arr)
+        fields += [z]
+    x_now = jnp.concatenate([*reversed(fields)], axis=1)
+    near = axis_index(mesh_dim)
+    return jnp.roll(x_now, (near + 1) * z.shape[1], axis=1)
+
+
+supply_islands = functools.partial(tiles_bind, mesh_dim="mp")
 
 
 def shifted(value, axis, steps):
@@ -81,7 +99,7 @@
     chosen = (owners == wanted)[:, None, None]
     taken = jnp.where(chosen, shard_piece[0], jnp.zeros_like(shard_piece[0]))
     image_part = jnp.sum(taken.astype(jnp.float32), axis=0).astype(jnp.bfloat16)
-    image = lax.all_gather(image_part, "mp", axis=1, tiled=True)
+    image = supply_islands(image_part)
     width_k = key_full.shape[1]
     keys_raw = jnp.dot(image, key_full, preferred_element_type=jnp.float32).reshape(
         slot_rows, width_k // HD, HD

time: 706 us -> 656 us (0.929)
  waiting for transfers between devices: 561 us -> 485 us
  local copies, waits for them, and re-layouts: 51.3 us -> 66.2 us
    ppermute x0 -> x3, waiting for transfers between devices: none -> 79 us  [tiles_bind(): z = ppermute(z, mesh_dim, perm=left_arr)]
    all_gather x1 -> x0, waiting for transfers between devices: 76.4 us -> none  [per_device(): image = lax.all_gather(image_part, 'mp', axis=1, tiled=True)]
    all_gather x1, waiting for transfers between devices: 140 us -> 85.6 us  [per_device(): full_text = lax.all_gather(arrived, 'mp', axis=3, tiled=True)[0, 0]]
    all_gather x1, waiting for transfers between devices: 34.7 us -> 0.02 us  [per_device(): shard_piece = lax.all_gather(vision, 'section', axis=1, tiled=True)]
    ppermute x1, waiting for transfers between devices: 47.3 us -> 68.3 us  [shifted(): return lax.ppermute(value, axis, pairs)]
    unnamed x40 -> x43, local copies, waits for them, and re-layouts: 6.98 us -> 19.9 us
  transfers between devices with their start and end apart: 10 -> 12, of which waited for: 9 -> 9; matrix products, arithmetic and copies ran while one was open for 10% -> 13% of each run, Pallas kernels for 0% -> 0%
where the time goes in v1:
time: 656 us; the launch traced here: 654 us
  waiting for transfers between devices  485 us (74%)
  local copies, waits for them, and re-layouts  66.2 us (10%)
  matrix products  50.2 us (8%)
  other arithmetic  29.4 us (4%)
  between operations  17.8 us (3%)
    all_gather x1, waiting for transfers between devices, per_device(): lax.all_gather(query_weight, 'dp', axis=1, tiled=True)[0]  100 us
    all_gather x1, waiting for transfers between devices, per_device(): full_text = lax.all_gather(arrived, 'mp', axis=3, tiled=True)[0, 0]  85.6 us
    ppermute x3, waiting for transfers between devices, tiles_bind(): z = ppermute(z, mesh_dim, perm=left_arr)  79 us
    ppermute x1, waiting for transfers between devices, shifted(): return lax.ppermute(value, axis, pairs)  68.3 us
    reduce_scatter x1, waiting for transfers between devices, per_device(): lax.psum_scatter(jnp.concatenate([key_part, value_part], axis=1).astype(j...  62.2 us
    reduce_scatter x1, waiting for transfers between devices, per_device(): lax.psum_scatter(partial_bf.astype(jnp.float32).astype(jnp.bfloat16), 'mp...  57 us
    reduce_scatter x1, waiting for transfers between devices, per_device(): lax.psum_scatter(jnp.where((row_ids // slot_rows == wanted)[:, None], tak...  30.4 us
    dot_general x1, local copies, waits for them, and re-layouts, per_device(): jnp.dot(columns, lax.all_gather(query_weight, 'dp', axis=1, tiled=True)[0...  21.4 us
  transfers between devices with their start and end apart: 12, of which 9 were waited for; matrix products, arithmetic and copies ran while one was open for 13% of the time, Pallas kernels for 0%

profile of v1, /device:TPU:0, one launch (start us, length us, event | category | flops | bytes accessed | tf_op | source)
XLA Modules:
  0.0 654.3 jit_solution(2992196396561804734)
XLA Ops:
  9.4 3.0 collective-permute-start.3
  12.4 68.3 %collective-permute-done.3 = bf16[1,1,512,2048]{3,2,1,0:T(8,128)(2,1)S(1)} collective-permute-done((bf16[1,1,512,2048]{3,2,1,0:T(8,128)(2,1)}, bf16[1,1,512,2048]{3,2,1,0:T(8,128)(2,1)S(1)}, u32[]{:S(2)}, u32[]{:S(2)}) %collective-permute-start.3) | collective-permute-done | bytes 2097184 | tf_op jit(solution)/shard_map/ppermute | solution.py:31
  84.1 2.5 fusion.38
  86.5 1.9 collective-permute-start
  88.4 24.3 %collective-permute-done = bf16[256,2048]{1,0:T(8,128)(2,1)S(1)} collective-permute-done((bf16[256,2048]{1,0:T(8,128)(2,1)S(1)}, bf16[256,2048]{1,0:T(8,128)(2,1)S(1)}, u32[]{:S(2)}, u32[]{:S(2)}) %collective-permute-start) | collective-permute-done | bytes 1048608 | tf_op jit(solution)/shard_map/ppermute | solution.py:18
  113.7 25.3 %collective-permute-done.1 = bf16[256,2048]{1,0:T(8,128)(2,1)} collective-permute-done((bf16[256,2048]{1,0:T(8,128)(2,1)S(1)}, bf16[256,2048]{1,0:T(8,128)(2,1)}, u32[]{:S(2)}, u32[]{:S(2)}) %collective-permute-start.1) | collective-permute-done | bytes 1048608 | tf_op jit(solution)/shard_map/ppermute | solution.py:18
  145.7 29.4 %collective-permute-done.2 = bf16[256,2048]{1,0:T(8,128)(2,1)} collective-permute-done((bf16[256,2048]{1,0:T(8,128)(2,1)}, bf16[256,2048]{1,0:T(8,128)(2,1)}, u32[]{:S(2)}, u32[]{:S(2)}) %collective-permute-start.2) | collective-permute-done | bytes 1048608 | tf_op jit(solution)/shard_map/ppermute | solution.py:18
  175.0 2.3 constant_dynamic-update-slice_fusion.7
  177.4 2.3 constant_dynamic-update-slice_fusion.6
  181.7 2.3 constant_dynamic-update-slice_fusion.3
  184.0 2.3 constant_dynamic-update-slice_fusion.2
  188.3 6.4 copy.51
  194.7 4.8 multiply_reduce_fusion.2
  200.3 6.4 copy.50
  206.7 4.7 fusion.64
  211.4 2.1 fusion.47
  213.6 85.6 %all-gather.12.cloned.1.call-done = bf16[1,1,512,8192]{3,2,1,0:T(8,128)(2,1)} async-done(((bf16[1,1,512,2048]{3,2,1,0:T(8,128)(2,1)}), bf16[1,1,512,8192]{3,2,1,0:T(8,128)(2,1)}) %all-gather.12.cloned.1.call-update) | async-done | bytes 8388624 | tf_op jit(solution)/shard_map/all_gather | solution.py:75
  299.1 5.1 fusion.1
  304.2 100.4 %all-gather.14.cloned.1.call-done = bf16[1,8192,1024]{2,1,0:T(8,128)(2,1)} async-done(((bf16[1,2048,1024]{2,1,0:T(8,128)(2,1)}), bf16[1,8192,1024]{2,1,0:T(8,128)(2,1)}) %all-gather.14.cloned.1.call-update) | async-done | bytes 16777232 | tf_op jit(solution)/shard_map/all_gather | solution.py:82
  404.6 21.4 %copy.52 = bf16[1024,8192]{1,0:T(8,128)(2,1)} copy(bf16[1024,8192]{0,1:T(8,128)(2,1)} %bitcast.148) | data formatting | bytes 33554432 | tf_op jit(solution)/shard_map/dot_general | solution.py:80
  426.0 14.8 %multiply_reduce_fusion = (f32[512,8]{0,1:T(8,128)S(1)}, f32[512,8,128]{0,2,1:T(8,128)S(1)}) fusion(bf16[8,128,8192]{2,1,0:T(8,128)(2,1)} %bitcast.149, bf16[1,1,512,8192]{3,2,1,0:T(8,128)(2,1)} %all-gather.12.cloned.1.call-done, f32[8192]{0:T(1024)S(1)} %bitcast.167, f32[512]{0:T(512)S(1)} %add_rsqrt_fusion.1), kind=kOutput, calls=%fused_computation.59 | convolution fusion | flops 8607756288 | bytes 27314176 | tf_op jit(solution)/shard_map/dot_general | solution.py:80
  441.3 5.1 fusion.109
  447.2 3.9 fusion.16
  457.4 3.4 fusion.4
  460.9 5.4 convolution_convert_fusion
  466.3 6.0 convolution_convert_fusion.1
  472.4 7.7 %pad_maximum_fusion = bf16[8192,512]{0,1:T(8,128)(2,1)} fusion(bf16[8192,256]{0,1:T(8,128)(2,1)} %convolution_convert_fusion, bf16[8192,256]{0,1:T(8,128)(2,1)} %convolution_convert_fusion.1), kind=kLoop, calls=%fused_computation.13 | loop fusion | flops 16777216 | bytes 16777216 | tf_op jit(solution)/shard_map/concatenate | solution.py:148
  480.8 57.0 %reduce-scatter.4.cloned.1.call-done = bf16[256,2048]{1,0:T(8,128)(2,1)} async-done(((bf16[256,8192]{1,0:T(8,128)(2,1)}), bf16[256,2048]{1,0:T(8,128)(2,1)}) %reduce-scatter.4.cloned.1.call-update) | async-done | bytes 1048592 | tf_op jit(solution)/shard_map/reduce_scatter | solution.py:127
  537.8 6.8 %gather_fusion = bf16[512,2048]{1,0:T(8,128)(2,1)} fusion(bf16[256,2048]{1,0:T(8,128)(2,1)} %reduce-scatter.4.cloned.1.call-done, s32[1024]{0:T(1024)S(1)} %pad_clamp_fusion), kind=kCustom, calls=%fused_computation | custom fusion | bytes 4196352 | tf_op jit(solution)/shard_map/jit(_take)/gather | solution.py:131
  544.6 3.7 select_convert_fusion
  550.6 62.2 %reduce-scatter.8.cloned.1.call-done = bf16[2048,512]{0,1:T(8,128)(2,1)} async-done(((bf16[8192,512]{0,1:T(8,128)(2,1)}), bf16[2048,512]{0,1:T(8,128)(2,1)}) %reduce-scatter.8.cloned.1.call-update) | async-done | bytes 2097168 | tf_op jit(solution)/shard_map/reduce_scatter | solution.py:147
  617.1 30.4 %reduce-scatter.6.cloned.1.call-done = bf16[256,2048]{1,0:T(8,128)(2,1)} async-done(((bf16[512,2048]{1,0:T(8,128)(2,1)}), bf16[256,2048]{1,0:T(8,128)(2,1)}) %reduce-scatter.6.cloned.1.call-update) | async-done | bytes 1048592 | tf_op jit(solution)/shard_map/reduce_scatter | solution.py:132
  (88 shorter events, 29.5 us)
Async XLA Ops:
  7.2 75.6 %copy-start = (s32[1,2]{1,0:T(1,128)S(1)}, s32[1,2]{1,0:T(1,128)}, u32[]{:S(2)}) copy-start(s32[1,2]{1,0:T(1,128)} %param.17) | copy-start | bytes 28
  7.2 76.9 %all-gather.6.cloned.1.call-start = ((), (), s32[]{:S(2)}) async-start(), calls=%async_computation.3 | async-start | bytes 3145728 | tf_op jit(solution)/shard_map/all_gather | solution.py:97
  7.9 180.4 %all-gather.10.cloned.1.call-start = ((), (), s32[]{:S(2)}) async-start(), calls=%async_computation.5 | async-start | bytes 5242880 | tf_op jit(solution)/shard_map/all_gather | solution.py:89
  8.7 191.6 %all-gather.8.cloned.1.call-start = ((), (), s32[]{:S(2)}) async-start(), calls=%async_computation.4 | async-start | bytes 5242880 | tf_op jit(solution)/shard_map/all_gather | solution.py:90
  9.4 289.7 %all-gather.12.cloned.1.call-start = ((), (), s32[]{:S(2)}) async-start(), calls=%async_computation.6 | async-start | bytes 10485760 | tf_op jit(solution)/shard_map/all_gather | solution.py:75
  9.4 71.3 %collective-permute-start.3 = (bf16[1,1,512,2048]{3,2,1,0:T(8,128)(2,1)}, bf16[1,1,512,2048]{3,2,1,0:T(8,128)(2,1)S(1)}, u32[]{:S(2)}, u32[]{:S(2)}) collective-permute-start(bf16[1,1,512,2048]{3,2,1,0:T(8,128)(2,1)} %param.13), channel_id=1, source_target_pairs={{0,16},{16,0},{1,17},{17,1},{2,18},{18,2},{3,19},{19,3},{4,20},{20... | collective-permute-start | bytes 6291464 | tf_op jit(solution)/shard_map/ppermute | solution.py:31
  80.8 1.3 copy-start.10
  82.1 322.5 %all-gather.14.cloned.1.call-start = ((), (), s32[]{:S(2)}) async-start(), calls=%async_computation.7 | async-start | bytes 20971520 | tf_op jit(solution)/shard_map/all_gather | solution.py:82
  82.7 61.1 %copy-start.15 = (s32[1,2]{1,0:T(1,128)S(1)}, s32[1,2]{1,0:T(1,128)}, u32[]{:S(2)}) copy-start(s32[1,2]{1,0:T(1,128)} %param.15) | copy-start | bytes 28
  82.7 455.1 %reduce-scatter.4.cloned.1.call-start = ((), (), s32[]{:S(2)}) async-start(), calls=%async_computation.8 | async-start | bytes 5242880 | tf_op jit(solution)/shard_map/reduce_scatter | solution.py:127
  86.5 26.2 %collective-permute-start = (bf16[256,2048]{1,0:T(8,128)(2,1)S(1)}, bf16[256,2048]{1,0:T(8,128)(2,1)S(1)}, u32[]{:S(2)}, u32[]{:S(2)}) collective-permute-start(bf16[256,2048]{1,0:T(8,128)(2,1)S(1)} %fusion.38), channel_id=1, source_target_pairs={{0,4},{4,8},{8,12},{12,0},{1,5},{5,9},{9,13},{13,1},{2,6},{6,10},{... | collective-permute-start | bytes 3145736 | tf_op jit(solution)/shard_map/ppermute | solution.py:18
  112.7 1.0 copy-start.8
  113.7 25.3 %collective-permute-start.1 = (bf16[256,2048]{1,0:T(8,128)(2,1)S(1)}, bf16[256,2048]{1,0:T(8,128)(2,1)}, u32[]{:S(2)}, u32[]{:S(2)}) collective-permute-start(bf16[256,2048]{1,0:T(8,128)(2,1)S(1)} %collective-permute-done), channel_id=1, source_target_pairs={{0,4},{4,8},{8,12},{12,0},{1,5},{5,9},{9,13},{13,1},{2,6},{6,10},{... | collective-permute-start | bytes 3145736 | tf_op jit(solution)/shard_map/ppermute | solution.py:18
  139.0 36.0 %collective-permute-start.2 = (bf16[256,2048]{1,0:T(8,128)(2,1)}, bf16[256,2048]{1,0:T(8,128)(2,1)}, u32[]{:S(2)}, u32[]{:S(2)}) collective-permute-start(bf16[256,2048]{1,0:T(8,128)(2,1)} %collective-permute-done.1), channel_id=1, source_target_pairs={{0,4},{4,8},{8,12},{12,0},{1,5},{5,9},{9,13},{13,1},{2,6},{6,10},{... | collective-permute-start | bytes 3145736 | tf_op jit(solution)/shard_map/ppermute | solution.py:18
  144.4 35.2 %copy-start.9 = (bf16[256,2048]{1,0:T(8,128)(2,1)S(1)}, bf16[256,2048]{1,0:T(8,128)(2,1)}, u32[]{:S(2)}) copy-start(bf16[256,2048]{1,0:T(8,128)(2,1)} %copy-done.8) | copy-start | bytes 3145732
  194.7 4.8 copy-start.12
  404.6 21.4 %copy-start.14 = (f32[1,8192]{1,0:T(1,128)S(1)}, f32[1,8192]{1,0:T(1,128)}, u32[]{:S(2)}) copy-start(f32[1,8192]{1,0:T(1,128)} %param.18) | copy-start | bytes 98308
  426.0 14.8 %copy-start.13 = (f32[1,128]{1,0:T(1,128)S(1)}, f32[1,128]{1,0:T(1,128)}, u32[]{:S(2)}) copy-start(f32[1,128]{1,0:T(1,128)} %param.22) | copy-start | bytes 1540
  447.2 3.9 copy-start.6
  447.2 4.7 copy-start.7
  447.2 4.7 copy-start.11
  447.2 4.7 copy-start.16
  451.1 2.3 copy-start.2
  453.1 2.2 copy-start.4
  455.3 2.2 copy-start.5
  460.9 151.9 %reduce-scatter.8.cloned.1.call-start = ((), (), s32[]{:S(2)}) async-start(), calls=%async_computation.10 | async-start | bytes 10485760 | tf_op jit(solution)/shard_map/reduce_scatter | solution.py:147
  480.1 167.4 %reduce-scatter.6.cloned.1.call-start = ((), (), s32[]{:S(2)}) async-start(), calls=%async_computation.9 | async-start | bytes 3145728 | tf_op jit(solution)/shard_map/reduce_scatter | solution.py:132
  544.6 3.7 copy-start.3
  549.4 98.1 %copy-start.1 = (s32[1,2]{1,0:T(1,128)S(1)}, s32[1,2]{1,0:T(1,128)}, u32[]{:S(2)}) copy-start(s32[1,2]{1,0:T(1,128)} %param.17) | copy-start | bytes 28
Sparse Core Ops, SparseCore 0:
  9.6 58.3 all-gather.5
  69.6 34.4 all-gather.9
  105.6 34.4 all-gather.7
  141.6 157.4 all-gather.11
  300.5 104.0 all-gather.13
  461.0 76.7 reduce-scatter.3
  540.5 72.2 reduce-scatter.7
  615.6 31.8 reduce-scatter.5
